TPU v7x, 32 devices: a whole 2x2x4 slice. The times are simulated.
32 devices in a mesh: groups: 2 (over y), ctx: 4 (over z), sub: 2 (over x), head: 2 (over core).
Axes of the slice: x: 2, y: 2, z: 4, core: 2. Of those that a mesh axis runs over, the one named last changes fastest.
Arguments:
- queries: bfloat16 [32, 10240, 128], P(('sub', 'head'), ('groups', 'ctx')), parts along dimension 1, may hold values from -6 to 6
- keys: bfloat16 [32, 10240, 128], P(('sub', 'head'), ('groups', 'ctx')), parts along dimension 1, may hold values from -6 to 6
- values: bfloat16 [32, 10240, 128], P(('sub', 'head'), ('groups', 'ctx')), parts along dimension 1, may hold values from -90 to 90
- out_grad: bfloat16 [32, 10240, 128], P(('sub', 'head'), ('groups', 'ctx')), parts along dimension 1, may hold values from -6 to 6
- norm_gain: float32 [32, 128], P(('sub', 'head')), may hold values from 0.25 to 1.75
- doc_ids: int32 [40], P(('groups', 'ctx')), parts along dimension 0, may hold values from 0 to 3, never falling along the last dimension, each value on 1 to 10 neighbouring positions
Outputs:
- grad_queries: bfloat16 [32, 10240, 128], P(('sub', 'head'), ('groups', 'ctx')), parts along dimension 1
- grad_keys: bfloat16 [32, 10240, 128], P(('sub', 'head'), ('groups', 'ctx')), parts along dimension 1
- grad_values: bfloat16 [32, 10240, 128], P(('sub', 'head'), ('groups', 'ctx')), parts along dimension 1
There are 2 independent parts, one for each index of `groups`. A program takes and returns all parts, laid end to end along the dimension named above; an argument that names none is the same for every part. Nothing has to cross between parts.
Inputs may be any that keep to these rules, and one draw needn't show every extreme that they name: `doc_ids`: never falls; each of its 4 values labels 1 to 10 consecutive blocks, one value exactly 10.
All inputs are finite; a program needn't handle non-finite values.
Results may differ from a plain program's by a relative error of at most 0.0058.
Values sent between devices are 32-bit elements; how exact they have to be, the bound alone decides.
No kernel may reach another device: no remote copies, remote signals or barrier semaphores. Data moves between devices by JAX's collectives and lax.ppermute only.
A program may use at most 128 MiB of HBM per device.

v0:
```python
import jax
import jax.numpy as jnp
from jax import lax
from jax.sharding import PartitionSpec as P


def carried_in(value, axis, combine, identity, reverse):
    peers, index = (lax.axis_size(axis), lax.axis_index(axis))
    everything = jax.tree.map(lambda part: lax.all_gather(part, axis), value)
    start = jax.tree.map(
        lambda part, zero: jnp.broadcast_to(jnp.asarray(zero, part.dtype), part.shape),
        value,
        identity,
    )

    def lap(k, before):
        at = peers - 1 - k if reverse else k
        reached = at > index if reverse else at < index
        new = combine(before, jax.tree.map(lambda part: part[at], everything))
        return jax.tree.map(lambda a, b: jnp.where(reached, a, b), new, before)

    return lax.fori_loop(0, peers, lap, start)


def carry_combine(earlier_part, later_part):
    joined = jnp.where(earlier_part[0] == later_part[0], 1.0, 0.0).astype(jnp.float32)
    return (later_part[0], later_part[1] + joined * earlier_part[1])


def on_device(queries, keys, values, out_grad, norm_gain, doc_ids):
    head_count, tok_count, head_width = queries.shape
    block_count = doc_ids.shape[0]
    block_len = tok_count // block_count
    block_shape = (head_count, block_count, block_len, head_width)
    highest_precision = lax.Precision.HIGHEST
    query_blocks = queries.reshape(block_shape)
    key_blocks = keys.reshape(block_shape)
    value_blocks = values.reshape(block_shape)
    row_ids = lax.broadcasted_iota(jnp.int32, (block_len, block_len), 0)
    col_ids = lax.broadcasted_iota(jnp.int32, (block_len, block_len), 1)
    causal = row_ids >= col_ids
    doc_values = doc_ids.astype(jnp.float32)
    block_pos = jnp.arange(block_count, dtype=jnp.int32)
    same_doc = doc_values[:, None] == doc_values[None, :]
    earlier_mask = (same_doc & (block_pos[None, :] < block_pos[:, None])).astype(jnp.float32)
    later_mask = (same_doc & (block_pos[None, :] > block_pos[:, None])).astype(jnp.float32)
    scores = jnp.einsum(
        "hnid,hnjd->hnij", query_blocks, key_blocks, preferred_element_type=jnp.float32
    )
    block_probs = jnp.where(causal, scores, 0.0).astype(jnp.bfloat16)
    intra_part = jnp.einsum(
        "hnij,hnjd->hnid", block_probs, value_blocks, preferred_element_type=jnp.float32
    )
    key_value_block = jnp.einsum(
        "hnid,hnie->hnde", key_blocks, value_blocks, preferred_element_type=jnp.float32
    )
    local_prefix = jnp.einsum(
        "bc,hcde->hbde", earlier_mask, key_value_block, precision=highest_precision
    )
    last_match = (doc_values == doc_values[-1]).astype(jnp.float32)
    device_kv = jnp.einsum("c,hcde->hde", last_match, key_value_block, precision=highest_precision)
    prior_doc, prior_state = carried_in(
        (doc_values[-1], device_kv),
        "ctx",
        carry_combine,
        (jnp.float32(-1.0), jnp.zeros_like(device_kv)),
        False,
    )
    prior_match = (doc_values == prior_doc).astype(jnp.float32)
    entering = prior_match[None, :, None, None] * prior_state[:, None, :, :]
    preceding_states = (local_prefix + entering).astype(jnp.bfloat16)
    cross_block_part = jnp.einsum(
        "hnid,hnde->hnie", query_blocks, preceding_states, preferred_element_type=jnp.float32
    )
    raw_attn = (intra_part + cross_block_part).reshape(head_count, tok_count, head_width)
    feature_count = head_count * head_width * lax.axis_size(("sub", "head"))
    scaled = norm_gain[:, None, :] * out_grad.astype(jnp.float32)
    square_total = lax.psum(jnp.sum(raw_attn * raw_attn, axis=(0, 2)), ("sub", "head"))
    root_mean = jnp.sqrt(square_total / feature_count + 1e-06)
    normed = raw_attn / root_mean[None, :, None]
    scaled_mean = lax.psum(jnp.sum(scaled * normed, axis=(0, 2)), ("sub", "head")) / feature_count
    d_attn = ((scaled - normed * scaled_mean[None, :, None]) / root_mean[None, :, None]).astype(
        jnp.bfloat16
    )
    output_grad_blocks = d_attn.reshape(block_shape)
    grad_scores = jnp.einsum(
        "hnid,hnjd->hnij", output_grad_blocks, value_blocks, preferred_element_type=jnp.float32
    )
    grad_probs = jnp.where(causal, grad_scores, 0.0).astype(jnp.bfloat16)
    query_gradient = jnp.einsum(
        "hnij,hnjd->hnid", grad_probs, key_blocks, preferred_element_type=jnp.float32
    )
    key_gradient = jnp.einsum(
        "hnij,hnid->hnjd", grad_probs, query_blocks, preferred_element_type=jnp.float32
    )
    value_gradient = jnp.einsum(
        "hnij,hnid->hnjd", block_probs, output_grad_blocks, preferred_element_type=jnp.float32
    )
    query_grad_block = jnp.einsum(
        "hnid,hnie->hnde", query_blocks, output_grad_blocks, preferred_element_type=jnp.float32
    )
    local_suffix = jnp.einsum(
        "bc,hcde->hbde", later_mask, query_grad_block, precision=highest_precision
    )
    first_match = (doc_values == doc_values[0]).astype(jnp.float32)
    device_qd = jnp.einsum(
        "c,hcde->hde", first_match, query_grad_block, precision=highest_precision
    )
    next_doc, next_state = carried_in(
        (doc_values[0], device_qd),
        "ctx",
        carry_combine,
        (jnp.float32(-1.0), jnp.zeros_like(device_qd)),
        True,
    )
    next_match = (doc_values == next_doc).astype(jnp.float32)
    leaving = next_match[None, :, None, None] * next_state[:, None, :, :]
    following_states = (local_suffix + leaving).astype(jnp.bfloat16)
    query_gradient = query_gradient + jnp.einsum(
        "hnie,hnde->hnid", output_grad_blocks, preceding_states, preferred_element_type=jnp.float32
    )
    key_gradient = key_gradient + jnp.einsum(
        "hnie,hnde->hnid", value_blocks, following_states, preferred_element_type=jnp.float32
    )
    value_gradient = value_gradient + jnp.einsum(
        "hnid,hnde->hnie", key_blocks, following_states, preferred_element_type=jnp.float32
    )
    out_shape = (head_count, tok_count, head_width)
    return (
        query_gradient.reshape(out_shape).astype(jnp.bfloat16),
        key_gradient.reshape(out_shape).astype(jnp.bfloat16),
        value_gradient.reshape(out_shape).astype(jnp.bfloat16),
    )


def solution(mesh):
    return jax.shard_map(
        on_device,
        mesh=mesh,
        in_specs=(
            P(("sub", "head"), ("groups", "ctx"), None),
            P(("sub", "head"), ("groups", "ctx"), None),
            P(("sub", "head"), ("groups", "ctx"), None),
            P(("sub", "head"), ("groups", "ctx"), None),
            P(("sub", "head"), None),
            P(("groups", "ctx")),
        ),
        out_specs=(
            P(("sub", "head"), ("groups", "ctx"), None),
            P(("sub", "head"), ("groups", "ctx"), None),
            P(("sub", "head"), ("groups", "ctx"), None),
        ),
        check_vma=False,
    )
```

profile of v0, /device:TPU:0, one launch (start us, length us, event | category | flops | bytes accessed | tf_op | source)
XLA Modules:
  0.0 199.0 jit_solution(3285715845271670284)
XLA Ops:
  9.3 3.4 %fusion.30 = f32[8,5,128,128]{3,2,1,0:T(8,128)S(1)} fusion(bf16[8,5,256,128]{3,2,1,0:T(8,128)(2,1)} %bitcast.118, bf16[8,5,256,128]{3,2,1,0:T(8,128)(2,1)} %bitcast.122), kind=kOutput, calls=%fused_computation.55 | convolution fusion | flops 335544320 | bytes 7864320 | tf_op jit(solution)/shard_map/hnid,hnie->hnde/dot_general | solution.py:54
  14.2 4.8 %fusion.4 = f32[1,8,128,128]{3,0,2,1:T(1,128)} fusion(f32[8,5,128,128]{3,2,1,0:T(8,128)S(1)} %fusion.30, f32[]{:T(128)} %bitcast.8, s32[5]{0:T(128)S(1)} %copy-done.15), kind=kOutput, calls=%fused_computation.17 | convolution fusion | flops 7864330 | bytes 3145752 | tf_op jit(solution)/shard_map/c,hcde->hde/dot_general | solution.py:61
  19.9 13.7 %all-reduce.2 = (f32[4]{0:T(128)S(1)}, f32[4]{0:T(128)S(1)}) all-reduce(f32[4]{0:T(128)S(1)} %get-tuple-element.341, f32[4]{0:T(128)S(1)} %slice_dynamic-update-slice_fusion), channel_id=1, replica_groups=mesh['groups'=2,'ctx'=4,'sub'=2,'head'=2] {'ctx'}, use_global_device_ids=true, to_apply=%add | all-reduce | flops 8 | bytes 64
  33.6 7.4 %fusion.6 = f32[8,128,128,5]{2,3,1,0:T(8,128)} fusion(f32[8,5,128,128]{3,2,1,0:T(8,128)} %copy-done.1, f32[5]{0:T(128)S(1)} %convert_element_type.51), kind=kOutput, calls=%fused_computation.19 | convolution fusion | flops 39321676 | bytes 5242900 | tf_op jit(solution)/shard_map/bc,hcde->hbde/dot_general | solution.py:57
  41.0 1.5 select_convert_fusion.1
  42.5 2.3 %copy-done.4 = bf16[8,5,256,256]{3,2,1,0:T(8,128)(2,1)} copy-done((bf16[8,5,256,256]{3,2,1,0:T(8,128)(2,1)}, bf16[8,5,256,256]{3,2,1,0:T(8,128)(2,1)S(1)}, u32[]{:S(2)}) %copy-start.4) | copy-done | bytes 5242904
  44.8 3.9 %fusion.29 = f32[8,5,256,128]{3,2,1,0:T(8,128)} fusion(bf16[8,5,256,256]{3,2,1,0:T(8,128)(2,1)S(1)} %select_convert_fusion.1, bf16[8,5,256,128]{3,2,1,0:T(8,128)(2,1)S(1)} %bitcast.123), kind=kOutput, calls=%fused_computation.54 | convolution fusion | flops 671088640 | bytes 13107200 | tf_op jit(solution)/shard_map/hnij,hnjd->hnid/dot_general | solution.py:51
  48.7 19.1 %all-gather.5.cloned.1.call-done = f32[32,128,128]{2,1,0:T(8,128)} async-done(((f32[8,128,128]{2,1,0:T(8,128)}), f32[32,128,128]{2,1,0:T(8,128)}) %all-gather.5.cloned.1.call-update) | async-done | bytes 2097168 | tf_op jit(solution)/shard_map/all_gather | solution.py:9
  67.8 13.5 %while.34 = (s32[]{:T(128)}, f32[]{:T(128)}, f32[8,128,128]{2,1,0:T(8,128)S(1)}, s32[]{:T(128)}, f32[4]{0:T(128)S(1)}, /*index=5*/f32[4,8,128,128]{3,2,1,0:T(8,128)}, s32[]{:T(128)}, f32[]{:T(128)}, f32[]{:T(128)}, s32[]{:T(128)}) while((s32[]{:T(128)}, f32[]{:T(128)}, f32[8,128,128]{2,1,0:T(8,128)S(1)}, s32[]{:T(128)}, ...), condition=%wide.region_1.2_spmd.clone, body=%wide.region_0.1_spmd.clone.sunk | while | flops 524295 | bytes 1573048 | solution.py:22
  69.7 1.5 fusion.62
  73.1 1.5 fusion.62
  81.4 3.0 %fusion.9 = bf16[8,5,128,128]{3,2,1,0:T(8,128)(2,1)S(1)} fusion(f32[8,128,128,5]{2,3,1,0:T(8,128)} %fusion.6, f32[8,128,128]{2,1,0:T(8,128)S(1)} %get-tuple-element.269, f32[5]{0:T(128)S(1)} %compare_convert_fusion.1), kind=kLoop, calls=%fused_computation.24 | loop fusion | flops 1966080 | bytes 4456468 | tf_op jit(solution)/shard_map/convert_element_type | solution.py:71
  85.2 3.2 %multiply_reduce_fusion.1 = (f32[5,256]{1,0:T(8,128)S(1)}, f32[8,5,256,128]{3,2,1,0:T(8,128)}) fusion(f32[8,5,256,128]{3,2,1,0:T(8,128)S(1)} %copy-done.5, bf16[8,5,256,128]{3,2,1,0:T(8,128)(2,1)S(1)} %bitcast.109, bf16[8,5,128,128]{3,2,1,0:T(8,128)(2,1)S(1)} %fusion.9), kind=kOutput, calls=%fused_computation.15 | convolution fusion | flops 339475200 | bytes 14423040 | tf_op jit(solution)/shard_map/hnid,hnde->hnie/dot_general | solution.py:72
  88.4 7.0 %psum.14 = f32[1280]{0:T(1024)S(1)} all-reduce(f32[1280]{0:T(1024)S(1)} %reduce_sum.21), channel_id=1, replica_groups=mesh['groups'=2,'ctx'=4,'sub'=2,'head'=2] {'sub','head'}, use_global_device_ids=true, to_apply=%region_3.4 | all-reduce | flops 1280 | bytes 10240 | tf_op jit(solution)/shard_map/psum | solution.py:78
  95.4 4.3 %multiply_reduce_fusion = f32[1280]{0:T(1024)S(1)} fusion(bf16[8,1280,128]{2,1,0:T(8,128)(2,1)} %param.13, f32[8,128]{1,0:T(8,128)S(1)} %copy-done.14, f32[1280]{0:T(1024)S(1)} %add_sqrt_fusion, f32[8,5,256,128]{3,2,1,0:T(8,128)} %get-tuple-element.344), kind=kLoop, calls=%fused_computation.14 | loop fusion | flops 6552320 | bytes 7878656 | tf_op jit(solution)/shard_map/reduce_sum | solution.py:81
  99.7 6.0 %psum.15 = f32[1280]{0:T(1024)S(1)} all-reduce(f32[1280]{0:T(1024)S(1)} %multiply_reduce_fusion), channel_id=1, replica_groups=mesh['groups'=2,'ctx'=4,'sub'=2,'head'=2] {'sub','head'}, use_global_device_ids=true, to_apply=%region_5.6 | all-reduce | flops 1280 | bytes 10240 | tf_op jit(solution)/shard_map/psum | solution.py:81
  105.7 4.1 %divide_convert_fusion = bf16[8,1280,128]{2,1,0:T(8,128)(2,1)S(1)} fusion(bf16[8,1280,128]{2,1,0:T(8,128)(2,1)} %param.13, f32[1280]{0:T(1024)S(1)} %broadcast_multiply_fusion, f32[1280]{0:T(1024)S(1)} %add_sqrt_fusion, f32[8,128]{1,0:T(8,128)S(1)} %copy-done.14, f32[8,5,256,128]{3,2,1,0:T(8,128)} %get-tuple-element.344), kind=kLoop, calls=%fused_computation.13 | loop fusion | flops 9175040 | bytes 10500096 | tf_op jit(solution)/shard_map/convert_element_type | solution.py:82
  109.9 1.5 copy-done.2
  111.4 2.4 %convolution_bitcast_fusion = f32[8,5,128,128]{2,3,1,0:T(8,128)} fusion(bf16[8,5,256,128]{3,2,1,0:T(8,128)(2,1)S(1)} %bitcast.112, bf16[8,5,256,128]{3,2,1,0:T(8,128)(2,1)S(1)} %bitcast.111), kind=kOutput, calls=%fused_computation.25 | convolution fusion | flops 335544320 | bytes 7864320 | tf_op jit(solution)/shard_map/hnid,hnie->hnde/dot_general | solution.py:99
  113.7 4.8 %copy.42 = f32[8,5,128,128]{3,1,2,0:T(8,128)} copy(f32[8,5,128,128]{2,3,1,0:T(8,128)} %convolution_bitcast_fusion) | data formatting | bytes 5242880 | tf_op jit(solution)/shard_map/hnid,hnie->hnde/dot_general | solution.py:99
  118.5 5.7 %fusion.19 = f32[1,8,128,128]{3,0,2,1:T(1,128)} fusion(f32[8,5,128,128]{3,1,2,0:T(8,128)} %copy.42, f32[]{:T(128)} %bitcast.23, s32[5]{0:T(128)S(1)} %copy-done.15), kind=kOutput, calls=%fused_computation.40 | convolution fusion | flops 7864330 | bytes 3145752 | tf_op jit(solution)/shard_map/c,hcde->hde/dot_general | solution.py:106
  124.3 6.6 %fusion.13 = f32[8,128,128,5]{2,3,1,0:T(8,128)} fusion(f32[8,5,128,128]{3,1,2,0:T(8,128)} %copy.42, f32[5]{0:T(128)S(1)} %convert_element_type.51), kind=kOutput, calls=%fused_computation.35 | convolution fusion | flops 39321676 | bytes 5242900 | tf_op jit(solution)/shard_map/bc,hcde->hbde/dot_general | solution.py:102
  130.8 1.5 select_convert_fusion
  132.6 1.5 fusion.31
  134.1 2.4 %add_convert_fusion = bf16[8,5,256,128]{3,2,1,0:T(8,128)(2,1)} fusion(f32[8,5,256,128]{3,2,1,0:T(8,128)S(1)} %fusion.31, bf16[8,5,256,128]{3,2,1,0:T(8,128)(2,1)S(1)} %bitcast.114, bf16[8,5,128,128]{3,2,1,0:T(8,128)(2,1)S(1)} %copy-done.13), kind=kOutput, calls=%fused_computation.12 | convolution fusion | flops 338165760 | bytes 11796480 | tf_op jit(solution)/shard_map/hnie,hnde->hnid/dot_general | solution.py:119
  136.6 3.9 %fusion.33 = f32[8,5,256,128]{3,2,1,0:T(8,128)} fusion(bf16[8,5,256,256]{3,2,1,0:T(8,128)(2,1)S(1)} %bitcast.117, bf16[8,5,256,128]{3,2,1,0:T(8,128)(2,1)S(1)} %bitcast.115), kind=kOutput, calls=%fused_computation.58 | convolution fusion | flops 671088640 | bytes 13107200 | tf_op jit(solution)/shard_map/hnij,hnid->hnjd/dot_general | solution.py:96
  140.5 3.9 %fusion.32 = f32[8,5,256,128]{3,2,1,0:T(8,128)} fusion(bf16[8,5,256,256]{3,2,1,0:T(8,128)(2,1)S(1)} %select_convert_fusion, bf16[8,5,256,128]{3,2,1,0:T(8,128)(2,1)S(1)} %bitcast.110), kind=kOutput, calls=%fused_computation.57 | convolution fusion | flops 671088640 | bytes 13107200 | tf_op jit(solution)/shard_map/hnij,hnid->hnjd/dot_general | solution.py:93
  144.4 23.7 %all-gather.7.cloned.1.call-done = f32[32,128,128]{2,1,0:T(8,128)} async-done(((f32[8,128,128]{2,1,0:T(8,128)}), f32[32,128,128]{2,1,0:T(8,128)}) %all-gather.7.cloned.1.call-update) | async-done | bytes 2097168 | tf_op jit(solution)/shard_map/all_gather | solution.py:9
  168.1 13.6 %while.35 = (s32[]{:T(128)}, f32[]{:T(128)}, f32[8,128,128]{2,1,0:T(8,128)S(1)}, s32[]{:T(128)}, f32[4]{0:T(128)S(1)}, /*index=5*/f32[4,8,128,128]{3,2,1,0:T(8,1...) while((s32[]{:T(128)}, f32[]{:T(128)}, ...), condition=%wide.region_7.8_spmd.clone, body=%wide.region_6.7_spmd.clone.sunk | while | flops 524299 | bytes 1573110 | solution.py:22
  181.7 3.0 %fusion.8 = bf16[8,5,128,128]{3,2,1,0:T(8,128)(2,1)S(1)} fusion(f32[8,128,128,5]{2,3,1,0:T(8,128)} %fusion.13, f32[8,128,128]{2,1,0:T(8,128)S(1)} %get-tuple-element.271, f32[5]{0:T(128)S(1)} %compare_convert_fusion), kind=kLoop, calls=%fused_computation.22 | loop fusion | flops 1966080 | bytes 4456468 | tf_op jit(solution)/shard_map/convert_element_type | solution.py:118
  184.7 5.1 %fusion.2 = bf16[8,5,256,128]{3,2,1,0:T(8,128)(2,1)} fusion(f32[8,5,256,128]{3,2,1,0:T(8,128)} %fusion.33, bf16[8,5,256,128]{3,2,1,0:T(8,128)(2,1)S(1)} %bitcast.121, bf16[8,5,128,128]{3,2,1,0:T(8,128)(2,1)S(1)} %fusion.8), kind=kOutput, calls=%fused_computation.7 | convolution fusion | flops 338165760 | bytes 11796480 | tf_op jit(solution)/shard_map/hnid,hnde->hnie/dot_general | solution.py:125
  189.9 2.3 %fusion.3 = bf16[8,5,256,128]{3,2,1,0:T(8,128)(2,1)} fusion(f32[8,5,256,128]{3,2,1,0:T(8,128)S(1)} %bitcast.127, bf16[8,5,128,128]{3,2,1,0:T(8,128)(2,1)S(1)} %fusion.8, bf16[8,5,256,128]{3,2,1,0:T(8,128)(2,1)S(1)} %bitcast.125), kind=kOutput, calls=%fused_computation.9 | convolution fusion | flops 338165760 | bytes 11796480 | tf_op jit(solution)/shard_map/hnie,hnde->hnid/dot_general | solution.py:122
  (72 shorter events, 19.1 us)
Async XLA Ops:
  7.2 33.8 %copy-start = (bf16[8,1280,128]{2,1,0:T(8,128)(2,1)S(1)}, bf16[8,1280,128]{2,1,0:T(8,128)(2,1)}, u32[]{:S(2)}) copy-start(bf16[8,1280,128]{2,1,0:T(8,128)(2,1)} %param.10) | copy-start | bytes 7864324
  7.2 60.7 %all-gather.5.cloned.1.call-start = ((), (), s32[]{:S(2)}) async-start(), calls=%async_computation | async-start | bytes 2621440 | tf_op jit(solution)/shard_map/all_gather | solution.py:9
  9.3 4.9 %copy-start.15 = (s32[5]{0:T(128)S(1)}, s32[5]{0:T(128)}, u32[]{:S(2)}) copy-start(s32[5]{0:T(128)} %param.15) | copy-start | bytes 64
  12.7 1.5 copy-start.1
  19.0 149.1 %all-gather.7.cloned.1.call-start = ((), (), s32[]{:S(2)}) async-start(), calls=%async_computation.1 | async-start | bytes 2621440 | tf_op jit(solution)/shard_map/all_gather | solution.py:9
  33.6 7.4 %copy-start.6 = (bf16[8,1280,128]{2,1,0:T(8,128)(2,1)S(1)}, bf16[8,1280,128]{2,1,0:T(8,128)(2,1)}, u32[]{:S(2)}) copy-start(bf16[8,1280,128]{2,1,0:T(8,128)(2,1)} %param.11) | copy-start | bytes 7864324
  41.0 3.9 %copy-start.9 = (bf16[8,1280,128]{2,1,0:T(8,128)(2,1)S(1)}, bf16[8,1280,128]{2,1,0:T(8,128)(2,1)}, u32[]{:S(2)}) copy-start(bf16[8,1280,128]{2,1,0:T(8,128)(2,1)} %param.12) | copy-start | bytes 7864324
  42.5 2.3 %copy-start.4 = (bf16[8,5,256,256]{3,2,1,0:T(8,128)(2,1)}, bf16[8,5,256,256]{3,2,1,0:T(8,128)(2,1)S(1)}, u32[]{:S(2)}) copy-start(bf16[8,5,256,256]{3,2,1,0:T(8,128)(2,1)S(1)} %select_convert_fusion.1) | copy-start | bytes 15728644
  81.4 3.7 %copy-start.5 = (f32[8,5,256,128]{3,2,1,0:T(8,128)S(1)}, f32[8,5,256,128]{3,2,1,0:T(8,128)}, u32[]{:S(2)}) copy-start(f32[8,5,256,128]{3,2,1,0:T(8,128)} %fusion.29) | copy-start | bytes 15728644
  85.2 3.2 %copy-start.12 = (bf16[8,5,128,128]{3,2,1,0:T(8,128)(2,1)}, bf16[8,5,128,128]{3,2,1,0:T(8,128)(2,1)S(1)}, u32[]{:S(2)}) copy-start(bf16[8,5,128,128]{3,2,1,0:T(8,128)(2,1)S(1)} %fusion.9) | copy-start | bytes 3932164
  85.2 10.3 %copy-start.14 = (f32[8,128]{1,0:T(8,128)S(1)}, f32[8,128]{1,0:T(8,128)}, u32[]{:S(2)}) copy-start(f32[8,128]{1,0:T(8,128)} %param.14) | copy-start | bytes 12292
  109.9 1.5 copy-start.2
  124.2 6.6 %copy-start.3 = (bf16[8,1280,128]{2,1,0:T(8,128)(2,1)S(1)}, bf16[8,1280,128]{2,1,0:T(8,128)(2,1)}, u32[]{:S(2)}) copy-start(bf16[8,1280,128]{2,1,0:T(8,128)(2,1)} %copy-done.2) | copy-start | bytes 7864324
  124.2 6.6 %copy-start.10 = (bf16[8,1280,128]{2,1,0:T(8,128)(2,1)S(1)}, bf16[8,1280,128]{2,1,0:T(8,128)(2,1)}, u32[]{:S(2)}) copy-start(bf16[8,1280,128]{2,1,0:T(8,128)(2,1)} %param.12) | copy-start | bytes 7864324
  130.8 1.7 copy-start.7
  130.8 5.7 %slice-start = ((s8[5242880]{0:T(1024)(128)(4,1)}), s8[4194304]{0:T(1024)(128)(4,1)S(1)}, s32[]{:S(2)}) async-start(s8[5242880]{0:T(1024)(128)(4,1)} %bitcast.116), calls=%async_computation.2 | async-start | bytes 8388608
  132.6 1.6 copy-start.13
  132.6 4.0 %slice-start.1 = ((s8[5242880]{0:T(1024)(128)(4,1)}), s8[1048576]{0:T(1024)(128)(4,1)S(1)}, s32[]{:S(2)}) async-start(s8[5242880]{0:T(1024)(128)(4,1)} %bitcast.116), calls=%async_computation.3 | async-start | bytes 2097152
  181.7 3.0 %copy-start.8 = (bf16[8,1280,128]{2,1,0:T(8,128)(2,1)S(1)}, bf16[8,1280,128]{2,1,0:T(8,128)(2,1)}, u32[]{:S(2)}) copy-start(bf16[8,1280,128]{2,1,0:T(8,128)(2,1)} %param.11) | copy-start | bytes 7864324
  181.7 8.1 %slice-start.2 = ((s8[5242880]{0:T(1024)(128)(4,1)}), s8[4194304]{0:T(1024)(128)(4,1)S(1)}, s32[]{:S(2)}) async-start(s8[5242880]{0:T(1024)(128)(4,1)} %bitcast.126), calls=%async_computation.4 | async-start | bytes 8388608
  184.7 5.1 %copy-start.11 = (bf16[8,1280,128]{2,1,0:T(8,128)(2,1)S(1)}, bf16[8,1280,128]{2,1,0:T(8,128)(2,1)}, u32[]{:S(2)}) copy-start(bf16[8,1280,128]{2,1,0:T(8,128)(2,1)} %param.12) | copy-start | bytes 7864324
  184.7 5.1 %slice-start.3 = ((s8[5242880]{0:T(1024)(128)(4,1)}), s8[1048576]{0:T(1024)(128)(4,1)S(1)}, s32[]{:S(2)}) async-start(s8[5242880]{0:T(1024)(128)(4,1)} %bitcast.126), calls=%async_computation.5 | async-start | bytes 2097152
Sparse Core Ops, SparseCore 0:
  19.2 48.6 all-gather.4
  124.3 43.7 all-gather.6
where the time goes:
time: 200 us; the launch traced here: 199 us
  matrix products  59.6 us (30%)
  waiting for transfers between devices  42.9 us (21%)
  other arithmetic  27 us (14%)
  blocking collectives  26.7 us (13%)
  local copies, waits for them, and re-layouts  17.8 us (9%)
  between operations  14.3 us (7%)
  loops' own time  10.6 us (5%)
    all_gather x2, waiting for transfers between devices, carried_in(): everything = jax.tree.map(lambda part: lax.all_gather(part, axis), value)  42.9 us
    unnamed x1, blocking collectives  13.7 us
    select_n x8, other arithmetic, lap(): return jax.tree.map(lambda a, b: jnp.where(reached, a, b), new, before)  11.8 us
    another operation x2, loops' own time, carried_in(): return lax.fori_loop(0, peers, lap, start)  10.6 us
    dot_general x1, matrix products, on_device(): jnp.einsum('bc,hcde->hbde', earlier_mask, key_value_block, precision=high...  7.38 us
    psum x1, blocking collectives, on_device(): lax.psum(jnp.sum(raw_attn * raw_attn, axis=(0, 2)), ('sub', 'head'))  7 us
    unnamed x44, local copies, waits for them, and re-layouts  6.97 us
    dot_general x1, matrix products, on_device(): jnp.einsum('bc,hcde->hbde', later_mask, query_grad_block, precision=highe...  6.56 us
  transfers between devices with their start and end apart: 2, of which 2 were waited for; matrix products, arithmetic and copies ran while one was open for 17% of the time, Pallas kernels for 0%

commit v1 on v0

--- a/solution.py
+++ b/solution.py
@@ -75,7 +75,9 @@
     raw_attn = (intra_part + cross_block_part).reshape(head_count, tok_count, head_width)
     feature_count = head_count * head_width * lax.axis_size(("sub", "head"))
     scaled = norm_gain[:, None, :] * out_grad.astype(jnp.float32)
-    square_total = lax.psum(jnp.sum(raw_attn * raw_attn, axis=(0, 2)), ("sub", "head"))
+    square_total = jnp.sum(
+        lax.all_gather(jnp.sum(raw_attn * raw_attn, axis=(0, 2)), ("sub", "head")), axis=0
+    )
     root_mean = jnp.sqrt(square_total / feature_count + 1e-06)
     normed = raw_attn / root_mean[None, :, None]
     scaled_mean = lax.psum(jnp.sum(scaled * normed, axis=(0, 2)), ("sub", "head")) / feature_count

time: 200 us -> 199 us (level)
    psum x1 -> x0, blocking collectives: 7 us -> none  [on_device(): lax.psum(jnp.sum(raw_attn * raw_attn, axis=(0, 2)), ('sub', 'head'))]
    all_gather x0 -> x1, blocking collectives: none -> 5.19 us  [on_device(): lax.all_gather(jnp.sum(raw_attn * raw_attn, axis=(0, 2)), ('sub', 'head'))]
    unnamed x44 -> x45, local copies, waits for them, and re-layouts: 6.97 us -> 6.98 us
where the time goes in v1:
time: 199 us; the launch traced here: 198 us
  matrix products  59.6 us (30%)
  waiting for transfers between devices  42.9 us (22%)
  other arithmetic  27.1 us (14%)
  blocking collectives  26 us (13%)
  local copies, waits for them, and re-layouts  17.8 us (9%)
  between operations  14.3 us (7%)
  loops' own time  10.6 us (5%)
    all_gather x2, waiting for transfers between devices, carried_in(): everything = jax.tree.map(lambda part: lax.all_gather(part, axis), value)  42.8 us
    unnamed x1, blocking collectives  13.7 us
    select_n x8, other arithmetic, lap(): return jax.tree.map(lambda a, b: jnp.where(reached, a, b), new, before)  11.8 us
    another operation x2, loops' own time, carried_in(): return lax.fori_loop(0, peers, lap, start)  10.6 us
    dot_general x1, matrix products, on_device(): jnp.einsum('bc,hcde->hbde', earlier_mask, key_value_block, precision=high...  7.38 us
    psum x1, blocking collectives, on_device(): lax.psum(jnp.sum(scaled * normed, axis=(0, 2)), ('sub', 'head'))  7.14 us
    unnamed x45, local copies, waits for them, and re-layouts  6.98 us
    dot_general x1, matrix products, on_device(): jnp.einsum('bc,hcde->hbde', later_mask, query_grad_block, precision=highe...  6.56 us
  transfers between devices with their start and end apart: 2, of which 2 were waited for; matrix products, arithmetic and copies ran while one was open for 17% of the time, Pallas kernels for 0%

profile of v1, /device:TPU:0, one launch (start us, length us, event | category | flops | bytes accessed | tf_op | source)
XLA Modules:
  0.0 198.4 jit_solution(11288232074622068356)
XLA Ops:
  9.3 3.4 %fusion.30 = f32[8,5,128,128]{3,2,1,0:T(8,128)S(1)} fusion(bf16[8,5,256,128]{3,2,1,0:T(8,128)(2,1)} %bitcast.118, bf16[8,5,256,128]{3,2,1,0:T(8,128)(2,1)} %bitcast.122), kind=kOutput, calls=%fused_computation.55 | convolution fusion | flops 335544320 | bytes 7864320 | tf_op jit(solution)/shard_map/hnid,hnie->hnde/dot_general | solution.py:54
  14.2 4.8 %fusion.4 = f32[1,8,128,128]{3,0,2,1:T(1,128)} fusion(f32[8,5,128,128]{3,2,1,0:T(8,128)S(1)} %fusion.30, f32[]{:T(128)} %bitcast.8, s32[5]{0:T(128)S(1)} %copy-done.15), kind=kOutput, calls=%fused_computation.17 | convolution fusion | flops 7864330 | bytes 3145752 | tf_op jit(solution)/shard_map/c,hcde->hde/dot_general | solution.py:61
  19.9 13.7 %all-reduce.2 = (f32[4]{0:T(128)S(1)}, f32[4]{0:T(128)S(1)}) all-reduce(f32[4]{0:T(128)S(1)} %get-tuple-element.341, f32[4]{0:T(128)S(1)} %slice_dynamic-update-slice_fusion), channel_id=1, replica_groups=mesh['groups'=2,'ctx'=4,'sub'=2,'head'=2] {'ctx'}, use_global_device_ids=true, to_apply=%add | all-reduce | flops 8 | bytes 64
  33.6 7.4 %fusion.6 = f32[8,128,128,5]{2,3,1,0:T(8,128)} fusion(f32[8,5,128,128]{3,2,1,0:T(8,128)} %copy-done.1, f32[5]{0:T(128)S(1)} %convert_element_type.51), kind=kOutput, calls=%fused_computation.19 | convolution fusion | flops 39321676 | bytes 5242900 | tf_op jit(solution)/shard_map/bc,hcde->hbde/dot_general | solution.py:57
  41.0 1.5 select_convert_fusion.1
  42.5 2.3 %copy-done.4 = bf16[8,5,256,256]{3,2,1,0:T(8,128)(2,1)} copy-done((bf16[8,5,256,256]{3,2,1,0:T(8,128)(2,1)}, bf16[8,5,256,256]{3,2,1,0:T(8,128)(2,1)S(1)}, u32[]{:S(2)}) %copy-start.4) | copy-done | bytes 5242904
  44.8 3.9 %fusion.29 = f32[8,5,256,128]{3,2,1,0:T(8,128)} fusion(bf16[8,5,256,256]{3,2,1,0:T(8,128)(2,1)S(1)} %select_convert_fusion.1, bf16[8,5,256,128]{3,2,1,0:T(8,128)(2,1)S(1)} %bitcast.123), kind=kOutput, calls=%fused_computation.54 | convolution fusion | flops 671088640 | bytes 13107200 | tf_op jit(solution)/shard_map/hnij,hnjd->hnid/dot_general | solution.py:51
  48.7 19.1 %all-gather.6.cloned.1.call-done = f32[32,128,128]{2,1,0:T(8,128)} async-done(((f32[8,128,128]{2,1,0:T(8,128)}), f32[32,128,128]{2,1,0:T(8,128)}) %all-gather.6.cloned.1.call-update) | async-done | bytes 2097168 | tf_op jit(solution)/shard_map/all_gather | solution.py:9
  67.8 13.5 %while.34 = (s32[]{:T(128)}, f32[]{:T(128)}, f32[8,128,128]{2,1,0:T(8,128)S(1)}, s32[]{:T(128)}, f32[4]{0:T(128)S(1)}, /*index=5*/f32[4,8,128,128]{3,2,1,0:T(8,128)}, s32[]{:T(128)}, f32[]{:T(128)}, f32[]{:T(128)}, s32[]{:T(128)}) while((s32[]{:T(128)}, f32[]{:T(128)}, f32[8,128,128]{2,1,0:T(8,128)S(1)}, s32[]{:T(128)}, ...), condition=%wide.region_1.2_spmd.clone, body=%wide.region_0.1_spmd.clone.sunk | while | flops 524295 | bytes 1573048 | solution.py:22
  69.7 1.5 fusion.62
  73.1 1.5 fusion.62
  81.4 3.0 %fusion.9 = bf16[8,5,128,128]{3,2,1,0:T(8,128)(2,1)S(1)} fusion(f32[8,128,128,5]{2,3,1,0:T(8,128)} %fusion.6, f32[8,128,128]{2,1,0:T(8,128)S(1)} %get-tuple-element.269, f32[5]{0:T(128)S(1)} %compare_convert_fusion.1), kind=kLoop, calls=%fused_computation.24 | loop fusion | flops 1966080 | bytes 4456468 | tf_op jit(solution)/shard_map/convert_element_type | solution.py:71
  85.2 3.2 %multiply_reduce_fusion.1 = (f32[5,256]{1,0:T(8,128)S(1)}, f32[8,5,256,128]{3,2,1,0:T(8,128)}) fusion(f32[8,5,256,128]{3,2,1,0:T(8,128)S(1)} %copy-done.5, bf16[8,5,256,128]{3,2,1,0:T(8,128)(2,1)S(1)} %bitcast.109, bf16[8,5,128,128]{3,2,1,0:T(8,128)(2,1)S(1)} %fusion.9), kind=kOutput, calls=%fused_computation.15 | convolution fusion | flops 339475200 | bytes 14423040 | tf_op jit(solution)/shard_map/hnid,hnde->hnie/dot_general | solution.py:72
  88.4 5.2 %all-gather.2 = f32[4,1,1280]{2,1,0:T(1,128)S(1)} all-gather(f32[1,1,1280]{2,1,0:T(1,128)S(1)} %reshape.55), channel_id=1, replica_groups=mesh['groups'=2,'ctx'=4,'sub'=2,'head'=2] {'sub','head'}, dimensions={0}, use_global_device_ids=true | all-gather | bytes 25600 | tf_op jit(solution)/shard_map/all_gather | solution.py:79
  93.7 4.3 %multiply_reduce_fusion = f32[1280]{0:T(1024)S(1)} fusion(bf16[8,1280,128]{2,1,0:T(8,128)(2,1)} %param.13, f32[8,128]{1,0:T(8,128)S(1)} %copy-done.14, f32[1280]{0:T(1024)S(1)} %add_sqrt_fusion, f32[8,5,256,128]{3,2,1,0:T(8,128)} %get-tuple-element.344), kind=kLoop, calls=%fused_computation.14 | loop fusion | flops 6552320 | bytes 7878656 | tf_op jit(solution)/shard_map/reduce_sum | solution.py:83
  97.9 7.1 %psum.7 = f32[1280]{0:T(1024)S(1)} all-reduce(f32[1280]{0:T(1024)S(1)} %multiply_reduce_fusion), channel_id=1, replica_groups=mesh['groups'=2,'ctx'=4,'sub'=2,'head'=2] {'sub','head'}, use_global_device_ids=true, to_apply=%region_5.6 | all-reduce | flops 1280 | bytes 10240 | tf_op jit(solution)/shard_map/psum | solution.py:83
  105.1 4.1 %divide_convert_fusion = bf16[8,1280,128]{2,1,0:T(8,128)(2,1)S(1)} fusion(bf16[8,1280,128]{2,1,0:T(8,128)(2,1)} %param.13, f32[1280]{0:T(1024)S(1)} %broadcast_multiply_fusion, f32[1280]{0:T(1024)S(1)} %add_sqrt_fusion, f32[8,128]{1,0:T(8,128)S(1)} %copy-done.14, f32[8,5,256,128]{3,2,1,0:T(8,128)} %get-tuple-element.344), kind=kLoop, calls=%fused_computation.13 | loop fusion | flops 9175040 | bytes 10500096 | tf_op jit(solution)/shard_map/convert_element_type | solution.py:84
  109.2 1.5 copy-done.2
  110.7 2.4 %convolution_bitcast_fusion = f32[8,5,128,128]{2,3,1,0:T(8,128)} fusion(bf16[8,5,256,128]{3,2,1,0:T(8,128)(2,1)S(1)} %bitcast.112, bf16[8,5,256,128]{3,2,1,0:T(8,128)(2,1)S(1)} %bitcast.111), kind=kOutput, calls=%fused_computation.25 | convolution fusion | flops 335544320 | bytes 7864320 | tf_op jit(solution)/shard_map/hnid,hnie->hnde/dot_general | solution.py:101
  113.1 4.8 %copy.42 = f32[8,5,128,128]{3,1,2,0:T(8,128)} copy(f32[8,5,128,128]{2,3,1,0:T(8,128)} %convolution_bitcast_fusion) | data formatting | bytes 5242880 | tf_op jit(solution)/shard_map/hnid,hnie->hnde/dot_general | solution.py:101
  117.9 5.7 %fusion.19 = f32[1,8,128,128]{3,0,2,1:T(1,128)} fusion(f32[8,5,128,128]{3,1,2,0:T(8,128)} %copy.42, f32[]{:T(128)} %bitcast.23, s32[5]{0:T(128)S(1)} %copy-done.15), kind=kOutput, calls=%fused_computation.40 | convolution fusion | flops 7864330 | bytes 3145752 | tf_op jit(solution)/shard_map/c,hcde->hde/dot_general | solution.py:108
  123.6 6.6 %fusion.13 = f32[8,128,128,5]{2,3,1,0:T(8,128)} fusion(f32[8,5,128,128]{3,1,2,0:T(8,128)} %copy.42, f32[5]{0:T(128)S(1)} %convert_element_type.51), kind=kOutput, calls=%fused_computation.35 | convolution fusion | flops 39321676 | bytes 5242900 | tf_op jit(solution)/shard_map/bc,hcde->hbde/dot_general | solution.py:104
  130.2 1.5 select_convert_fusion
  131.9 1.5 fusion.31
  133.5 2.4 %add_convert_fusion = bf16[8,5,256,128]{3,2,1,0:T(8,128)(2,1)} fusion(f32[8,5,256,128]{3,2,1,0:T(8,128)S(1)} %fusion.31, bf16[8,5,256,128]{3,2,1,0:T(8,128)(2,1)S(1)} %bitcast.114, bf16[8,5,128,128]{3,2,1,0:T(8,128)(2,1)S(1)} %copy-done.13), kind=kOutput, calls=%fused_computation.12 | convolution fusion | flops 338165760 | bytes 11796480 | tf_op jit(solution)/shard_map/hnie,hnde->hnid/dot_general | solution.py:121
  135.9 3.9 %fusion.33 = f32[8,5,256,128]{3,2,1,0:T(8,128)} fusion(bf16[8,5,256,256]{3,2,1,0:T(8,128)(2,1)S(1)} %bitcast.117, bf16[8,5,256,128]{3,2,1,0:T(8,128)(2,1)S(1)} %bitcast.115), kind=kOutput, calls=%fused_computation.58 | convolution fusion | flops 671088640 | bytes 13107200 | tf_op jit(solution)/shard_map/hnij,hnid->hnjd/dot_general | solution.py:98
  139.8 3.9 %fusion.32 = f32[8,5,256,128]{3,2,1,0:T(8,128)} fusion(bf16[8,5,256,256]{3,2,1,0:T(8,128)(2,1)S(1)} %select_convert_fusion, bf16[8,5,256,128]{3,2,1,0:T(8,128)(2,1)S(1)} %bitcast.110), kind=kOutput, calls=%fused_computation.57 | convolution fusion | flops 671088640 | bytes 13107200 | tf_op jit(solution)/shard_map/hnij,hnid->hnjd/dot_general | solution.py:95
  143.7 23.7 %all-gather.8.cloned.1.call-done = f32[32,128,128]{2,1,0:T(8,128)} async-done(((f32[8,128,128]{2,1,0:T(8,128)}), f32[32,128,128]{2,1,0:T(8,128)}) %all-gather.8.cloned.1.call-update) | async-done | bytes 2097168 | tf_op jit(solution)/shard_map/all_gather | solution.py:9
  167.5 13.6 %while.35 = (s32[]{:T(128)}, f32[]{:T(128)}, f32[8,128,128]{2,1,0:T(8,128)S(1)}, s32[]{:T(128)}, f32[4]{0:T(128)S(1)}, /*index=5*/f32[4,8,128,128]{3,2,1,0:T(8,1...) while((s32[]{:T(128)}, f32[]{:T(128)}, ...), condition=%wide.region_7.8_spmd.clone, body=%wide.region_6.7_spmd.clone.sunk | while | flops 524299 | bytes 1573110 | solution.py:22
  181.1 3.0 %fusion.8 = bf16[8,5,128,128]{3,2,1,0:T(8,128)(2,1)S(1)} fusion(f32[8,128,128,5]{2,3,1,0:T(8,128)} %fusion.13, f32[8,128,128]{2,1,0:T(8,128)S(1)} %get-tuple-element.271, f32[5]{0:T(128)S(1)} %compare_convert_fusion), kind=kLoop, calls=%fused_computation.22 | loop fusion | flops 1966080 | bytes 4456468 | tf_op jit(solution)/shard_map/convert_element_type | solution.py:120
  184.1 5.1 %fusion.2 = bf16[8,5,256,128]{3,2,1,0:T(8,128)(2,1)} fusion(f32[8,5,256,128]{3,2,1,0:T(8,128)} %fusion.33, bf16[8,5,256,128]{3,2,1,0:T(8,128)(2,1)S(1)} %bitcast.121, bf16[8,5,128,128]{3,2,1,0:T(8,128)(2,1)S(1)} %fusion.8), kind=kOutput, calls=%fused_computation.7 | convolution fusion | flops 338165760 | bytes 11796480 | tf_op jit(solution)/shard_map/hnid,hnde->hnie/dot_general | solution.py:127
  189.2 2.3 %fusion.3 = bf16[8,5,256,128]{3,2,1,0:T(8,128)(2,1)} fusion(f32[8,5,256,128]{3,2,1,0:T(8,128)S(1)} %bitcast.127, bf16[8,5,128,128]{3,2,1,0:T(8,128)(2,1)S(1)} %fusion.8, bf16[8,5,256,128]{3,2,1,0:T(8,128)(2,1)S(1)} %bitcast.125), kind=kOutput, calls=%fused_computation.9 | convolution fusion | flops 338165760 | bytes 11796480 | tf_op jit(solution)/shard_map/hnie,hnde->hnid/dot_general | solution.py:124
  (73 shorter events, 19.1 us)
Async XLA Ops:
  7.2 33.8 %copy-start = (bf16[8,1280,128]{2,1,0:T(8,128)(2,1)S(1)}, bf16[8,1280,128]{2,1,0:T(8,128)(2,1)}, u32[]{:S(2)}) copy-start(bf16[8,1280,128]{2,1,0:T(8,128)(2,1)} %param.10) | copy-start | bytes 7864324
  7.2 60.7 %all-gather.6.cloned.1.call-start = ((), (), s32[]{:S(2)}) async-start(), calls=%async_computation | async-start | bytes 2621440 | tf_op jit(solution)/shard_map/all_gather | solution.py:9
  9.3 4.9 %copy-start.15 = (s32[5]{0:T(128)S(1)}, s32[5]{0:T(128)}, u32[]{:S(2)}) copy-start(s32[5]{0:T(128)} %param.15) | copy-start | bytes 64
  12.7 1.5 copy-start.1
  19.0 148.4 %all-gather.8.cloned.1.call-start = ((), (), s32[]{:S(2)}) async-start(), calls=%async_computation.1 | async-start | bytes 2621440 | tf_op jit(solution)/shard_map/all_gather | solution.py:9
  33.6 7.4 %copy-start.6 = (bf16[8,1280,128]{2,1,0:T(8,128)(2,1)S(1)}, bf16[8,1280,128]{2,1,0:T(8,128)(2,1)}, u32[]{:S(2)}) copy-start(bf16[8,1280,128]{2,1,0:T(8,128)(2,1)} %param.11) | copy-start | bytes 7864324
  41.0 3.9 %copy-start.9 = (bf16[8,1280,128]{2,1,0:T(8,128)(2,1)S(1)}, bf16[8,1280,128]{2,1,0:T(8,128)(2,1)}, u32[]{:S(2)}) copy-start(bf16[8,1280,128]{2,1,0:T(8,128)(2,1)} %param.12) | copy-start | bytes 7864324
  42.5 2.3 %copy-start.4 = (bf16[8,5,256,256]{3,2,1,0:T(8,128)(2,1)}, bf16[8,5,256,256]{3,2,1,0:T(8,128)(2,1)S(1)}, u32[]{:S(2)}) copy-start(bf16[8,5,256,256]{3,2,1,0:T(8,128)(2,1)S(1)} %select_convert_fusion.1) | copy-start | bytes 15728644
  81.4 3.7 %copy-start.5 = (f32[8,5,256,128]{3,2,1,0:T(8,128)S(1)}, f32[8,5,256,128]{3,2,1,0:T(8,128)}, u32[]{:S(2)}) copy-start(f32[8,5,256,128]{3,2,1,0:T(8,128)} %fusion.29) | copy-start | bytes 15728644
  85.2 3.2 %copy-start.12 = (bf16[8,5,128,128]{3,2,1,0:T(8,128)(2,1)}, bf16[8,5,128,128]{3,2,1,0:T(8,128)(2,1)S(1)}, u32[]{:S(2)}) copy-start(bf16[8,5,128,128]{3,2,1,0:T(8,128)(2,1)S(1)} %fusion.9) | copy-start | bytes 3932164
  85.2 8.5 %copy-start.14 = (f32[8,128]{1,0:T(8,128)S(1)}, f32[8,128]{1,0:T(8,128)}, u32[]{:S(2)}) copy-start(f32[8,128]{1,0:T(8,128)} %param.14) | copy-start | bytes 12292
  109.2 1.5 copy-start.2
  123.6 6.6 %copy-start.3 = (bf16[8,1280,128]{2,1,0:T(8,128)(2,1)S(1)}, bf16[8,1280,128]{2,1,0:T(8,128)(2,1)}, u32[]{:S(2)}) copy-start(bf16[8,1280,128]{2,1,0:T(8,128)(2,1)} %copy-done.2) | copy-start | bytes 7864324
  123.6 6.6 %copy-start.10 = (bf16[8,1280,128]{2,1,0:T(8,128)(2,1)S(1)}, bf16[8,1280,128]{2,1,0:T(8,128)(2,1)}, u32[]{:S(2)}) copy-start(bf16[8,1280,128]{2,1,0:T(8,128)(2,1)} %param.12) | copy-start | bytes 7864324
  130.2 1.7 copy-start.7
  130.2 5.7 %slice-start = ((s8[5242880]{0:T(1024)(128)(4,1)}), s8[4194304]{0:T(1024)(128)(4,1)S(1)}, s32[]{:S(2)}) async-start(s8[5242880]{0:T(1024)(128)(4,1)} %bitcast.116), calls=%async_computation.2 | async-start | bytes 8388608
  131.9 1.6 copy-start.13
  131.9 4.0 %slice-start.1 = ((s8[5242880]{0:T(1024)(128)(4,1)}), s8[1048576]{0:T(1024)(128)(4,1)S(1)}, s32[]{:S(2)}) async-start(s8[5242880]{0:T(1024)(128)(4,1)} %bitcast.116), calls=%async_computation.3 | async-start | bytes 2097152
  181.0 3.0 %copy-start.8 = (bf16[8,1280,128]{2,1,0:T(8,128)(2,1)S(1)}, bf16[8,1280,128]{2,1,0:T(8,128)(2,1)}, u32[]{:S(2)}) copy-start(bf16[8,1280,128]{2,1,0:T(8,128)(2,1)} %param.11) | copy-start | bytes 7864324
  181.1 8.1 %slice-start.2 = ((s8[5242880]{0:T(1024)(128)(4,1)}), s8[4194304]{0:T(1024)(128)(4,1)S(1)}, s32[]{:S(2)}) async-start(s8[5242880]{0:T(1024)(128)(4,1)} %bitcast.126), calls=%async_computation.4 | async-start | bytes 8388608
  184.0 5.1 %copy-start.11 = (bf16[8,1280,128]{2,1,0:T(8,128)(2,1)S(1)}, bf16[8,1280,128]{2,1,0:T(8,128)(2,1)}, u32[]{:S(2)}) copy-start(bf16[8,1280,128]{2,1,0:T(8,128)(2,1)} %param.12) | copy-start | bytes 7864324
  184.1 5.1 %slice-start.3 = ((s8[5242880]{0:T(1024)(128)(4,1)}), s8[1048576]{0:T(1024)(128)(4,1)S(1)}, s32[]{:S(2)}) async-start(s8[5242880]{0:T(1024)(128)(4,1)} %bitcast.126), calls=%async_computation.5 | async-start | bytes 2097152
Sparse Core Ops, SparseCore 0:
  19.2 48.6 all-gather.5
  123.7 43.7 all-gather.7
